TPU v7x, 32 devices: a whole 2x2x4 slice. The times are simulated.
32 devices in a mesh: tm: 4 (over y, x), series: 8 (over z, core).
Axes of the slice: x: 2, y: 2, z: 4, core: 2. Of those that a mesh axis runs over, the one named last changes fastest.
Arguments:
- codes: int32 [8, 512], P(None, ('tm', 'series')), may hold values from 0 to 916478, as said below
- owner_slot: int32 [8], replicated, may hold values from 0 to 7, each once
- edges: int32 [4096], replicated, may hold values from 0 to 2096640, as said below
- w_in: bfloat16 [128, 2304], replicated, may hold values from -0.09375 to 0.09375
- w_dt: bfloat16 [128, 32], replicated, may hold values from -0.5 to 0.5
- dt_bias: float32 [32], replicated, may hold values from -1 to 1
- decay_rate: float32 [32], replicated, may hold values from 1e-05 to 0.1
- grad_out: bfloat16 [8, 512, 2048], P('series', 'tm'), may hold values from -6 to 6
Outputs:
- ssd_output: bfloat16 [8, 512, 2048], P('series', 'tm')
- grad_in: float32 [128, 2304], replicated
Inputs may be any that keep to these rules, and one draw needn't show every extreme that they name: `codes`: each row is one series in the order of ingestion slots. edges[0] is 0 and edges rise strictly.
All inputs are finite; a program needn't handle non-finite values.
Results may differ from a plain program's by a relative error of at most 0.0062.
The roundings to bfloat16 on the way count: a program that leaves them out, or rounds other values in their place, can miss the bound.
Values sent between devices are 32-bit elements; how exact they have to be, the bound alone decides.
No kernel may reach another device: no remote copies, remote signals or barrier semaphores. Data moves between devices by JAX's collectives and lax.ppermute only.
A program may use at most 128 MiB of HBM per device.

v0:
```python
import math
import jax
import jax.numpy as jnp
from jax import lax
from jax.sharding import PartitionSpec as P

code_ceiling = 2097152.0


def decay_matrix(cum_decay):
    row_count = cum_decay.shape[0]
    causal = jnp.arange(row_count)[:, None] >= jnp.arange(row_count)[None, :]
    log_span = cum_decay.T[:, :, None] - cum_decay.T[:, None, :]
    return jnp.where(causal[None], jnp.exp(jnp.where(causal[None], log_span, -60.0)), 0.0)


def on_device(codes, owner_slot, edges, w_in, w_dt, dt_bias, decay_rate, grad_out):
    fl = jnp.float32
    half = jnp.bfloat16
    tok_rows = grad_out.shape[1]
    head_count = dt_bias.shape[0]
    inner_width = grad_out.shape[2]
    head_dim = inner_width // head_count
    state_dim = (w_in.shape[1] - inner_width) // 2
    n_blocks = lax.axis_size("tm")
    seq_len = tok_rows * n_blocks
    series_count = lax.axis_size("series")
    my_block = lax.axis_index("tm")
    my_series = lax.axis_index("series")
    all_codes = lax.all_gather(codes, ("tm", "series"), axis=1, tiled=True)
    row = lax.dynamic_index_in_dim(all_codes, owner_slot[my_series], axis=0, keepdims=False)
    reading = row.astype(fl)
    edge_float = edges.astype(fl)
    upper_edge = jnp.concatenate([edge_float[1:], jnp.full((1,), code_ceiling, fl)])
    onehot = (
        (edge_float[None, :] <= reading[:, None]) & (upper_edge[None, :] > reading[:, None])
    ).astype(fl)
    counts = jnp.sum(onehot, axis=0)
    before = jnp.cumsum(counts) - counts
    bin_table = jnp.stack([before, counts, edge_float, upper_edge - edge_float], axis=1)
    picked = jnp.dot(onehot, bin_table, precision=lax.Precision.HIGHEST)
    within_bin = (reading - picked[:, 2]) / picked[:, 3]
    quantile = (picked[:, 0] + picked[:, 1] * within_bin) / seq_len
    frequency = (jnp.arange(w_in.shape[0], dtype=fl) + 0.5) * math.pi
    features_all = jnp.cos(quantile[:, None] * frequency).astype(half)
    projected_all = jnp.dot(features_all, w_in, preferred_element_type=fl).astype(half)
    projected_all = projected_all.reshape(n_blocks, tok_rows, -1)
    x_all = projected_all[:, :, :inner_width].reshape(n_blocks, tok_rows, head_count, head_dim)
    b_all = projected_all[:, :, inner_width : inner_width + state_dim]
    c_all = projected_all[:, :, inner_width + state_dim :]
    step_all = jax.nn.softplus(
        dt_bias + jnp.dot(features_all, w_dt, preferred_element_type=fl)
    ).reshape(n_blocks, tok_rows, head_count)
    cum_all = jnp.cumsum(-step_all * decay_rate, axis=1)
    gate_all = jnp.exp(cum_all[:, -1])
    tail_all = jnp.exp(cum_all[:, -1:, :] - cum_all) * step_all
    xw_all = (x_all * tail_all[..., None]).astype(half)
    state_local_all = jnp.einsum("bthp,btn->bhpn", xw_all, b_all, preferred_element_type=fl)
    state_in = jnp.zeros((head_count, head_dim, state_dim), fl)
    for k in range(n_blocks - 1):
        new = gate_all[k][:, None, None] * state_in + state_local_all[k]
        state_in = jnp.where(k < my_block, new, state_in)

    def mine(a):
        return lax.dynamic_index_in_dim(a, my_block, axis=0, keepdims=False)

    features = mine(features_all.reshape(n_blocks, tok_rows, -1))
    x_heads = mine(x_all)
    b_proj = mine(b_all)
    c_proj = mine(c_all)
    step_size = mine(step_all)
    cum_decay = mine(cum_all)
    tail_factor = mine(tail_all)
    x_weighted = mine(xw_all)
    head_factor = jnp.exp(cum_decay)
    grad_heads = grad_out[0].reshape(tok_rows, head_count, head_dim)
    grad_weighted = (grad_heads * head_factor[:, :, None]).astype(half)
    adjoint_local = jnp.einsum("thp,tn->hpn", grad_weighted, c_proj, preferred_element_type=fl)
    adjoint_all = lax.all_gather(adjoint_local, "tm")
    adjoint_in = jnp.zeros((head_count, head_dim, state_dim), fl)
    for k in range(n_blocks - 1, 0, -1):
        new = gate_all[k][:, None, None] * adjoint_in + adjoint_all[k]
        adjoint_in = jnp.where(k > my_block, new, adjoint_in)
    masked = decay_matrix(cum_decay) * step_size.T[:, None, :]
    scores = jnp.dot(c_proj, b_proj.T, preferred_element_type=fl)
    weights = (scores[None] * masked).astype(half)
    state_half = state_in.astype(half)
    adjoint_half = adjoint_in.astype(half)
    output = jnp.einsum("hts,shp->thp", weights, x_heads, preferred_element_type=fl)
    output = (
        output
        + jnp.einsum("tn,hpn->thp", c_proj, state_half, preferred_element_type=fl)
        * head_factor[:, :, None]
    )
    ssd_output = output.reshape(1, tok_rows, inner_width).astype(half)
    grad_x = jnp.einsum("hts,thp->shp", weights, grad_heads, preferred_element_type=fl)
    grad_x = (
        grad_x
        + jnp.einsum("sn,hpn->shp", b_proj, adjoint_half, preferred_element_type=fl)
        * tail_factor[:, :, None]
    )
    pair_scores = jnp.einsum("thp,shp->hts", grad_heads, x_heads, preferred_element_type=fl)
    pair_mixed = jnp.sum(pair_scores * masked, axis=0).astype(half)
    grad_b = jnp.dot(pair_mixed.T, c_proj, preferred_element_type=fl)
    grad_b = grad_b + jnp.einsum("shp,hpn->sn", x_weighted, adjoint_half, preferred_element_type=fl)
    grad_c = jnp.dot(pair_mixed, b_proj, preferred_element_type=fl)
    grad_c = grad_c + jnp.einsum(
        "thp,hpn->tn", grad_weighted, state_half, preferred_element_type=fl
    )
    grad_rows = jnp.concatenate(
        [
            grad_x.reshape(tok_rows, inner_width).astype(half),
            grad_b.astype(half),
            grad_c.astype(half),
        ],
        axis=1,
    )
    local_grad = jnp.einsum("tf,tw->fw", features, grad_rows, preferred_element_type=fl)
    share_grad = lax.psum_scatter(local_grad, "series", scatter_dimension=1, tiled=True)
    share_grad = lax.psum(share_grad, "tm")
    total_grad = lax.all_gather(share_grad, "series", axis=1, tiled=True)
    grad_in = total_grad / math.sqrt(series_count * seq_len)
    return (ssd_output, grad_in)


def solution(mesh):
    return jax.shard_map(
        on_device,
        mesh=mesh,
        in_specs=(P(None, ("tm", "series")), P(), P(), P(), P(), P(), P(), P("series", "tm", None)),
        out_specs=(P("series", "tm", None), P()),
        check_vma=False,
    )
```

profile of v0, /device:TPU:0, one launch (start us, length us, event | category | flops | bytes accessed | tf_op | source)
XLA Modules:
  0.0 243.4 jit_solution(498775291195324287)
XLA Ops:
  7.2 0.0 all-gather.7.cloned.1.call-start
  7.2 1.3 dynamic_slice.34
  9.8 44.0 %all-gather.1 = s32[32,16,8]{1,2,0:T(8,128)S(1)} all-gather(s32[1,16,8]{1,2,0:T(8,128)} %bitcast.172), channel_id=1, replica_groups=mesh['tm'=4,'series'=8] {'tm','series'}, dimensions={0}, use_global_device_ids=true | all-gather | bytes 16896 | tf_op jit(solution)/shard_map/all_gather | solution.py:30
  53.8 0.1 reshape.163
  54.0 0.7 convert_element_type.97
  54.7 0.1 slice.91
  55.4 0.8 convert_subtract_fusion
  56.2 1.4 convert_reduce_fusion
  57.7 0.3 reduce-window.9
  58.0 0.1 slice.92
  58.0 0.1 reduce-window.12
  58.1 0.1 slice_reduce_fusion
  58.2 0.1 broadcast_add_fusion
  58.3 4.1 %fusion = f32[512,4]{0,1:T(4,128)S(1)} fusion(f32[4096]{0:T(1024)S(1)} %get-tuple-element.13, f32[4096]{0:T(1024)S(1)} %convert_element_type.97, f32[512]{0:T(512)S(1)} %bitcast.168, f32[4096,1]{0,1:T(1,128)S(1)} %bitcast.166, f32[4096,1]{0,1:T(1,128)S(1)} %bitcast.155, f32[4096,1]{0,1:T(1,128)S(1)} %bitcast.154, f32[4096,1]{0,1:T(1,128)S(1)} %sub.42), kind=kOutput, calls=%fused_computation.2 | convolution fusion | flops 107003904 | bytes 108544 | tf_op jit(solution)/shard_map/dot_general | solution.py:41
  62.5 1.6 convolution_convert_fusion
  64.2 1.1 compare_select_fusion
  65.3 0.1 copy.56
  65.5 0.7 negate_multiply_fusion
  66.2 1.2 reduce_window_sum.35
  67.4 0.8 fusion.97
  68.3 0.6 constant_dynamic-slice_fusion.3
  68.9 1.5 copy.57
  70.4 0.7 bitcast_exponential_fusion
  71.1 2.0 copy.61
  73.2 1.1 fusion.24
  74.3 0.8 copy-done.4
  75.1 2.0 fusion.59
  77.1 0.2 reduce-scatter.2.cloned.1.call-start
  77.4 1.6 slice.98
  79.0 0.5 slice.101
  79.6 3.2 %copy.54 = bf16[4,128,2048]{1,2,0:T(8,128)(2,1)S(1)} copy(bf16[4,128,2048]{2,1,0:T(8,128)(2,1)} %slice.98) | data formatting | bytes 4194304 | tf_op jit(solution)/shard_map/slice | solution.py:48
  82.8 1.2 exp.26
  84.0 1.7 exponential_multiply_fusion
  85.7 1.0 copy.60
  86.8 0.9 constant_dynamic-slice_fusion
  87.6 0.7 copy.64
  88.3 1.2 constant_dynamic-slice_fusion.1
  89.5 0.9 fusion.64
  90.4 1.4 multiply_bitcast_fusion
  91.9 2.4 fusion.4
  94.3 1.0 fusion.66
  95.3 1.0 fusion.62
  96.3 2.3 convolution_bitcast_fusion
  98.6 0.7 multiply_convert_fusion
  99.3 3.6 %fusion.41 = f32[4,32,64,128]{3,2,1,0:T(8,128)} fusion(bf16[4,128,32,64]{1,3,2,0:T(8,128)(2,1)S(1)} %multiply_convert_fusion, bf16[4,128,2304]{2,1,0:T(8,128)(2,1)} %bitcast.143), kind=kOutput, calls=%fused_computation.67 | convolution fusion | flops 268435456 | bytes 6422528 | tf_op jit(solution)/shard_map/bthp,btn->bhpn/dot_general | solution.py:58
  102.9 23.4 %all-gather.7.cloned.1.call-done = f32[128,64,128]{2,1,0:T(8,128)} async-done(((f32[32,64,128]{2,1,0:T(8,128)}), f32[128,64,128]{2,1,0:T(8,128)}) %all-gather.7.cloned.1.call-update) | async-done | bytes 4194320 | tf_op jit(solution)/shard_map/all_gather | solution.py:79
  126.3 3.6 %fusion.15 = (bf16[1,32,64,128]{3,2,1,0:T(8,128)(2,1)S(1)}, bf16[1,32,64,128]{3,2,1,0:T(8,128)(2,1)S(1)}) fusion(f32[128,64,128]{2,1,0:T(8,128)} %all-gather.7.cloned.1.call-done, f32[32]{0:T(128)S(1)} %copy-done.19, f32[32]{0:T(128)S(1)} %copy-done.21, f32[32]{0:T(128)S(1)} %copy-done.22, pred[]{:T(512)S(6)} %lt.34, pred[]{:T(512)S(6)} %lt.33, pred[]{:T(512)S(6)} %lt.32, ...), kind=kLoop, calls=%fused_computation.30 | loop fusion | flops 4718592 | bytes 7340550 | tf_op jit(solution)/shard_map/convert_element_type | solution.py:88
  130.0 0.3 fusion.11
  130.3 1.1 fusion.8
  131.4 0.4 fusion.12
  131.8 1.6 fusion.25
  133.4 0.0 reduce-scatter.2.cloned.1.call-update
  133.4 0.0 all-reduce.2.cloned.1.call-start
  133.5 32.8 %reduce-scatter.2.cloned.1.call-done = f32[128,288]{0,1:T(8,128)} async-done(((f32[128,2304]{0,1:T(8,128)}), f32[128,288]{0,1:T(8,128)}) %reduce-scatter.2.cloned.1.call-update) | async-done | bytes 147472 | tf_op jit(solution)/shard_map/reduce_scatter | solution.py:119
  166.2 0.0 all-reduce.2.cloned.1.call-update
  166.3 0.0 all-gather.5.cloned.1.call-start
  166.3 43.3 %all-reduce.2.cloned.1.call-done = f32[128,288]{0,1:T(8,128)} async-done(((f32[128,288]{0,1:T(8,128)}), f32[128,288]{0,1:T(8,128)}) %all-reduce.2.cloned.1.call-update) | async-done | bytes 147472 | tf_op jit(solution)/shard_map/psum | solution.py:120
  209.7 0.0 all-gather.5.cloned.1.call-update
  209.7 3.3 %convolution_bitcast_fusion.1 = f32[128,32,64]{0,2,1:T(8,128)S(1)} fusion(f32[32,128]{1,0:T(8,128)S(1)} %bitcast.165, f32[32,128]{1,0:T(8,128)S(1)} %bitcast.159, f32[128,128]{0,1:T(8,128)S(1)} %copy-done.13, pred[128,128]{0,1:T(8,128)(4,1)S(1)} %copy-done.17, bf16[4,128,32,64]{1,3,2,0:T(8,128)(2,1)} %bitcast.145, s32[]{:T(128)S(6)} %select_n.83), kind=kOutput, calls=%fused_computation.17 | convolution fusion | flops 70254592 | bytes 1703940 | tf_op jit(solution)/shard_map/hts,shp->thp/dot_general | solution.py:89
  213.0 1.1 fusion.7
  214.1 1.0 copy.65
  215.1 19.0 %all-gather.5.cloned.1.call-done = f32[128,2304]{0,1:T(8,128)} async-done(((f32[128,288]{0,1:T(8,128)}), f32[128,2304]{0,1:T(8,128)}) %all-gather.5.cloned.1.call-update) | async-done | bytes 1179664 | tf_op jit(solution)/shard_map/all_gather | solution.py:121
  234.1 1.3 broadcast_multiply_fusion
  235.5 1.4 copy.66
  (66 shorter events, 0.3 us)
Async XLA Ops:
  7.2 55.4 %copy-start = (bf16[128,2304]{1,0:T(8,128)(2,1)S(1)}, bf16[128,2304]{1,0:T(8,128)(2,1)}, u32[]{:S(2)}) copy-start(bf16[128,2304]{1,0:T(8,128)(2,1)} %param.11) | copy-start | bytes 1769476
  7.2 119.1 %all-gather.7.cloned.1.call-start = ((), (), s32[]{:S(2)}) async-start(), calls=%async_computation.4 | async-start | bytes 5242880 | tf_op jit(solution)/shard_map/all_gather | solution.py:79
  9.8 54.3 %copy-start.23 = (f32[128]{0:T(128)}, f32[128]{0:T(128)S(1)}, u32[]{:S(2)}) copy-start(f32[128]{0:T(128)S(1)} %add_multiply_fusion) | copy-start | bytes 1540
  62.4 1.7 copy-start.27
  62.5 1.7 copy-start.28
  62.5 3.0 %copy-start.25 = (f32[32]{0:T(128)S(1)}, f32[32]{0:T(128)}, u32[]{:S(2)}) copy-start(f32[32]{0:T(128)} %param.14) | copy-start | bytes 388
  62.5 2.8 %copy-start.18 = (f32[512,1]{0,1:T(1,128)}, f32[512,1]{0,1:T(1,128)S(1)}, u32[]{:S(2)}) copy-start(f32[512,1]{0,1:T(1,128)S(1)} %fusion.89) | copy-start | bytes 6148
  64.2 13.2 %copy-start.1 = (bf16[512,2304]{1,0:T(8,128)(2,1)}, bf16[512,2304]{1,0:T(8,128)(2,1)S(1)}, u32[]{:S(2)}) copy-start(bf16[512,2304]{1,0:T(8,128)(2,1)S(1)} %convolution_convert_fusion) | copy-start | bytes 7077892
  67.4 11.6 %copy-start.7 = (f32[4,128,32]{2,1,0:T(8,128)}, f32[4,128,32]{2,1,0:T(8,128)S(1)}, u32[]{:S(2)}) copy-start(f32[4,128,32]{2,1,0:T(8,128)S(1)} %reduce_window_sum.35) | copy-start | bytes 196612
  74.3 0.8 copy-start.4
  77.1 89.1 %reduce-scatter.2.cloned.1.call-start = ((), (), s32[]{:S(2)}) async-start(), calls=%async_computation.1 | async-start | bytes 1327104 | tf_op jit(solution)/shard_map/reduce_scatter | solution.py:119
  79.6 12.3 %copy-start.6 = (bf16[1,128,2048]{1,2,0:T(8,128)(2,1)S(1)}, bf16[1,128,2048]{1,2,0:T(8,128)(2,1)}, u32[]{:S(2)}) copy-start(bf16[1,128,2048]{1,2,0:T(8,128)(2,1)} %copy.61) | copy-start | bytes 1572868
  82.8 11.5 %copy-start.2 = (bf16[4,128,2048]{1,2,0:T(8,128)(2,1)}, bf16[4,128,2048]{1,2,0:T(8,128)(2,1)S(1)}, u32[]{:S(2)}) copy-start(bf16[4,128,2048]{1,2,0:T(8,128)(2,1)S(1)} %copy.54) | copy-start | bytes 6291460
  89.5 6.7 %copy-start.14 = (f32[1,128,32]{1,0,2:T(1,128)}, f32[1,128,32]{1,0,2:T(1,128)S(1)}, u32[]{:S(2)}) copy-start(f32[1,128,32]{1,0,2:T(1,128)S(1)} %constant_dynamic-slice_fusion.2) | copy-start | bytes 49156
  89.5 6.7 %copy-start.16 = (pred[128,128]{0,1:T(8,128)(4,1)}, pred[128,128]{0,1:T(8,128)(4,1)S(1)}, u32[]{:S(2)}) copy-start(pred[128,128]{0,1:T(8,128)(4,1)S(1)} %iota_compare_fusion) | copy-start | bytes 49156
  90.4 5.8 %copy-start.12 = (f32[128,128]{0,1:T(8,128)}, f32[128,128]{0,1:T(8,128)S(1)}, u32[]{:S(2)}) copy-start(f32[128,128]{0,1:T(8,128)S(1)} %fusion.64) | copy-start | bytes 196612
  91.9 4.4 %copy-start.10 = (f32[1,128,32]{1,2,0:T(8,128)S(1)}, f32[1,128,32]{1,2,0:T(8,128)}, u32[]{:S(2)}) copy-start(f32[1,128,32]{1,2,0:T(8,128)} %copy.57) | copy-start | bytes 49156
  96.3 2.4 copy-start.3
  99.3 27.0 %copy-start.19 = (f32[32]{0:T(128)S(1)}, f32[32]{0:T(128)}, u32[]{:S(2)}) copy-start(f32[32]{0:T(128)} %get-tuple-element.14) | copy-start | bytes 388
  99.3 27.0 %copy-start.20 = (f32[32]{0:T(128)S(1)}, f32[32]{0:T(128)}, u32[]{:S(2)}) copy-start(f32[32]{0:T(128)} %get-tuple-element.15) | copy-start | bytes 388
  99.3 27.0 %copy-start.21 = (f32[32]{0:T(128)S(1)}, f32[32]{0:T(128)}, u32[]{:S(2)}) copy-start(f32[32]{0:T(128)} %get-tuple-element.16) | copy-start | bytes 388
  99.3 27.0 %copy-start.22 = (f32[32]{0:T(128)S(1)}, f32[32]{0:T(128)}, u32[]{:S(2)}) copy-start(f32[32]{0:T(128)} %get-tuple-element.17) | copy-start | bytes 388
  126.3 4.0 %copy-start.8 = (f32[128,32,64]{0,2,1:T(8,128)S(1)}, f32[128,32,64]{0,2,1:T(8,128)}, u32[]{:S(2)}) copy-start(f32[128,32,64]{0,2,1:T(8,128)} %convolution_bitcast_fusion) | copy-start | bytes 3145732
  126.3 4.0 %copy-start.9 = (f32[1,128,32]{1,2,0:T(8,128)S(1)}, f32[1,128,32]{1,2,0:T(8,128)}, u32[]{:S(2)}) copy-start(f32[1,128,32]{1,2,0:T(8,128)} %copy.64) | copy-start | bytes 49156
  129.9 1.5 copy-start.5
  129.9 1.9 copy-start.24
  129.9 1.9 copy-start.26
  131.4 78.3 %copy-start.11 = (f32[1,128,32]{1,2,0:T(8,128)S(1)}, f32[1,128,32]{1,2,0:T(8,128)}, u32[]{:S(2)}) copy-start(f32[1,128,32]{1,2,0:T(8,128)} %copy.57) | copy-start | bytes 49156
  131.4 78.3 %copy-start.13 = (f32[128,128]{0,1:T(8,128)S(1)}, f32[128,128]{0,1:T(8,128)}, u32[]{:S(2)}) copy-start(f32[128,128]{0,1:T(8,128)} %copy-done.12) | copy-start | bytes 196612
  131.4 78.3 %copy-start.15 = (f32[1,128,32]{1,0,2:T(1,128)S(1)}, f32[1,128,32]{1,0,2:T(1,128)}, u32[]{:S(2)}) copy-start(f32[1,128,32]{1,0,2:T(1,128)} %copy-done.14) | copy-start | bytes 49156
  131.4 78.3 %copy-start.17 = (pred[128,128]{0,1:T(8,128)(4,1)S(1)}, pred[128,128]{0,1:T(8,128)(4,1)}, u32[]{:S(2)}) copy-start(pred[128,128]{0,1:T(8,128)(4,1)} %copy-done.16) | copy-start | bytes 49156
  133.4 76.2 %all-reduce.2.cloned.1.call-start = ((), (), s32[]{:S(2)}) async-start(), calls=%async_computation.2 | async-start | bytes 294912 | tf_op jit(solution)/shard_map/psum | solution.py:120
  166.3 67.8 %all-gather.5.cloned.1.call-start = ((), (), s32[]{:S(2)}) async-start(), calls=%async_computation.3 | async-start | bytes 1327104 | tf_op jit(solution)/shard_map/all_gather | solution.py:121
Sparse Core Ops, SparseCore 0:
  77.3 48.9 all-gather.6
  133.6 32.6 reduce-scatter.1
  169.2 40.4 all-reduce.1
  211.3 22.8 all-gather.4
where the time goes:
time: 245 us; the launch traced here: 243 us
  waiting for transfers between devices  119 us (49%)
  blocking collectives  44 us (18%)
  matrix products  27.7 us (11%)
  local copies, waits for them, and re-layouts  21.2 us (9%)
  between operations  16.2 us (7%)
  other arithmetic  15.3 us (6%)
    all_gather x1, blocking collectives, on_device(): all_codes = lax.all_gather(codes, ('tm', 'series'), axis=1, tiled=True)  44 us
    psum x1, waiting for transfers between devices, on_device(): share_grad = lax.psum(share_grad, 'tm')  43.3 us
    reduce_scatter x1, waiting for transfers between devices, on_device(): lax.psum_scatter(local_grad, 'series', scatter_dimension=1, tiled=True)  32.8 us
    all_gather x1, waiting for transfers between devices, on_device(): adjoint_all = lax.all_gather(adjoint_local, 'tm')  23.4 us
    all_gather x1, waiting for transfers between devices, on_device(): total_grad = lax.all_gather(share_grad, 'series', axis=1, tiled=True)  19 us
    unnamed x62, local copies, waits for them, and re-layouts  5.44 us
  transfers between devices with their start and end apart: 4, of which 4 were waited for; matrix products, arithmetic and copies ran while one was open for 13% of the time, Pallas kernels for 0%

commit v1 on v0

--- a/solution.py
+++ b/solution.py
@@ -118,7 +118,14 @@
     local_grad = jnp.einsum("tf,tw->fw", features, grad_rows, preferred_element_type=fl)
     share_grad = lax.psum_scatter(local_grad, "series", scatter_dimension=1, tiled=True)
     share_grad = lax.psum(share_grad, "tm")
-    total_grad = lax.all_gather(share_grad, "series", axis=1, tiled=True)
+    ring = [share_grad]
+    for hop in range(7):
+        ring.append(lax.ppermute(ring[-1], "series", [(dev, (dev + 1) % 8) for dev in range(8)]))
+    total_grad = jnp.roll(
+        jnp.concatenate(ring[::-1], axis=1),
+        (lax.axis_index("series") + 1) * ring[0].shape[1],
+        axis=1,
+    )
     grad_in = total_grad / math.sqrt(series_count * seq_len)
     return (ssd_output, grad_in)
 

time: 245 us -> 264 us (1.078)
  waiting for transfers between devices: 119 us -> 138 us
    ppermute x0 -> x7, waiting for transfers between devices: none -> 39.4 us  [on_device(): lax.ppermute(ring[-1], 'series', [(dev, (dev + 1) % 8) for dev in range(8)])]
    all_gather x1 -> x0, waiting for transfers between devices: 19 us -> none  [on_device(): total_grad = lax.all_gather(share_grad, 'series', axis=1, tiled=True)]
    unnamed x62 -> x81, local copies, waits for them, and re-layouts: 5.44 us -> 5.65 us
  transfers between devices with their start and end apart: 4 -> 10, of which waited for: 4 -> 10; matrix products, arithmetic and copies ran while one was open for 13% -> 12% of each run, Pallas kernels for 0% -> 0%
where the time goes in v1:
time: 264 us; the launch traced here: 263 us
  waiting for transfers between devices  138 us (52%)
  blocking collectives  44 us (17%)
  matrix products  28.4 us (11%)
  local copies, waits for them, and re-layouts  21.7 us (8%)
  between operations  16.4 us (6%)
  other arithmetic  14.1 us (5%)
    all_gather x1, blocking collectives, on_device(): all_codes = lax.all_gather(codes, ('tm', 'series'), axis=1, tiled=True)  44 us
    psum x1, waiting for transfers between devices, on_device(): share_grad = lax.psum(share_grad, 'tm')  43.2 us
    ppermute x7, waiting for transfers between devices, on_device(): lax.ppermute(ring[-1], 'series', [(dev, (dev + 1) % 8) for dev in range(8)])  39.4 us
    reduce_scatter x1, waiting for transfers between devices, on_device(): lax.psum_scatter(local_grad, 'series', scatter_dimension=1, tiled=True)  32.9 us
    all_gather x1, waiting for transfers between devices, on_device(): adjoint_all = lax.all_gather(adjoint_local, 'tm')  22.4 us
    unnamed x81, local copies, waits for them, and re-layouts  5.65 us
  transfers between devices with their start and end apart: 10, of which 10 were waited for; matrix products, arithmetic and copies ran while one was open for 12% of the time, Pallas kernels for 0%

profile of v1, /device:TPU:0, one launch (start us, length us, event | category | flops | bytes accessed | tf_op | source)
XLA Modules:
  0.0 262.8 jit_solution(9324722986071684134)
XLA Ops:
  7.2 1.3 dynamic_slice.38
  9.8 44.0 %all-gather.1 = s32[32,16,8]{1,2,0:T(8,128)S(1)} all-gather(s32[1,16,8]{1,2,0:T(8,128)} %bitcast.172), channel_id=1, replica_groups=mesh['tm'=4,'series'=8] {'tm','series'}, dimensions={0}, use_global_device_ids=true | all-gather | bytes 16896 | tf_op jit(solution)/shard_map/all_gather | solution.py:30
  53.8 0.1 reshape.163
  54.0 0.7 convert_element_type.97
  54.7 0.1 slice.91
  55.4 0.8 convert_subtract_fusion
  56.2 1.4 convert_reduce_fusion
  57.7 0.3 reduce-window.9
  58.0 0.1 slice.92
  58.0 0.1 reduce-window.12
  58.1 0.1 slice_reduce_fusion
  58.2 0.1 broadcast_add_fusion
  58.3 4.1 %fusion = f32[512,4]{0,1:T(4,128)S(1)} fusion(f32[4096]{0:T(1024)S(1)} %get-tuple-element.13, f32[4096]{0:T(1024)S(1)} %convert_element_type.97, f32[512]{0:T(512)S(1)} %bitcast.168, f32[4096,1]{0,1:T(1,128)S(1)} %bitcast.166, f32[4096,1]{0,1:T(1,128)S(1)} %bitcast.155, f32[4096,1]{0,1:T(1,128)S(1)} %bitcast.154, f32[4096,1]{0,1:T(1,128)S(1)} %sub.46), kind=kOutput, calls=%fused_computation.2 | convolution fusion | flops 107003904 | bytes 108544 | tf_op jit(solution)/shard_map/dot_general | solution.py:41
  62.5 1.6 convolution_convert_fusion
  64.2 1.1 compare_select_fusion
  65.3 0.1 copy.56
  65.5 0.7 negate_multiply_fusion
  66.2 1.2 reduce_window_sum.35
  67.4 0.8 fusion.97
  68.2 0.6 constant_dynamic-slice_fusion.3
  68.9 1.5 copy.57
  70.4 0.7 bitcast_exponential_fusion
  71.1 2.0 copy.61
  73.1 1.1 fusion.24
  74.3 0.8 copy-done.4
  75.1 2.0 fusion.59
  77.1 0.2 reduce-scatter.2.cloned.1.call-start
  77.4 1.6 slice.98
  79.0 0.6 slice.101
  79.6 3.2 %copy.54 = bf16[4,128,2048]{1,2,0:T(8,128)(2,1)S(1)} copy(bf16[4,128,2048]{2,1,0:T(8,128)(2,1)} %slice.98) | data formatting | bytes 4194304 | tf_op jit(solution)/shard_map/slice | solution.py:48
  82.8 1.4 exp.26
  84.2 1.7 exponential_multiply_fusion
  85.9 1.0 copy.60
  87.0 0.9 constant_dynamic-slice_fusion
  87.8 0.7 copy.64
  88.5 1.2 constant_dynamic-slice_fusion.1
  89.8 0.9 fusion.64
  90.7 1.4 multiply_bitcast_fusion
  92.2 2.4 fusion.4
  94.6 1.6 fusion.66
  96.2 1.0 fusion.62
  97.2 2.4 convolution_bitcast_fusion
  99.6 0.7 multiply_convert_fusion
  100.3 3.6 %fusion.41 = f32[4,32,64,128]{3,2,1,0:T(8,128)} fusion(bf16[4,128,32,64]{1,3,2,0:T(8,128)(2,1)S(1)} %multiply_convert_fusion, bf16[4,128,2304]{2,1,0:T(8,128)(2,1)} %bitcast.143), kind=kOutput, calls=%fused_computation.67 | convolution fusion | flops 268435456 | bytes 6422528 | tf_op jit(solution)/shard_map/bthp,btn->bhpn/dot_general | solution.py:58
  103.9 22.4 %all-gather.4.cloned.1.call-done = f32[128,64,128]{2,1,0:T(8,128)} async-done(((f32[32,64,128]{2,1,0:T(8,128)}), f32[128,64,128]{2,1,0:T(8,128)}) %all-gather.4.cloned.1.call-update) | async-done | bytes 4194320 | tf_op jit(solution)/shard_map/all_gather | solution.py:79
  126.3 3.6 %fusion.15 = (bf16[1,32,64,128]{3,2,1,0:T(8,128)(2,1)S(1)}, bf16[1,32,64,128]{3,2,1,0:T(8,128)(2,1)S(1)}) fusion(f32[128,64,128]{2,1,0:T(8,128)} %all-gather.4.cloned.1.call-done, f32[32]{0:T(128)S(1)} %copy-done.21, f32[32]{0:T(128)S(1)} %copy-done.23, f32[32]{0:T(128)S(1)} %copy-done.24, pred[]{:T(512)S(6)} %lt.46, pred[]{:T(512)S(6)} %lt.45, pred[]{:T(512)S(6)} %lt.44, ...), kind=kLoop, calls=%fused_computation.31 | loop fusion | flops 4718592 | bytes 7340550 | tf_op jit(solution)/shard_map/convert_element_type | solution.py:88
  130.0 0.3 fusion.11
  130.3 1.1 fusion.8
  131.5 0.3 fusion.12
  131.8 1.6 fusion.25
  133.5 32.9 %reduce-scatter.2.cloned.1.call-done = f32[128,288]{0,1:T(8,128)} async-done(((f32[128,2304]{0,1:T(8,128)}), f32[128,288]{0,1:T(8,128)}) %reduce-scatter.2.cloned.1.call-update) | async-done | bytes 147472 | tf_op jit(solution)/shard_map/reduce_scatter | solution.py:119
  166.5 43.2 %all-reduce.2.cloned.1.call-done = f32[128,288]{0,1:T(8,128)} async-done(((f32[128,288]{0,1:T(8,128)}), f32[128,288]{0,1:T(8,128)}) %all-reduce.2.cloned.1.call-update) | async-done | bytes 147472 | tf_op jit(solution)/shard_map/psum | solution.py:120
  209.6 6.6 %collective-permute-done = f32[128,288]{0,1:T(8,128)S(1)} collective-permute-done((f32[128,288]{0,1:T(8,128)}, f32[128,288]{0,1:T(8,128)S(1)}, u32[]{:S(2)}, u32[]{:S(2)}) %collective-permute-start) | collective-permute-done | bytes 147488 | tf_op jit(solution)/shard_map/ppermute | solution.py:123
  216.2 6.4 %collective-permute-done.1 = f32[128,288]{0,1:T(8,128)S(1)} collective-permute-done((f32[128,288]{0,1:T(8,128)S(1)}, f32[128,288]{0,1:T(8,128)S(1)}, u32[]{:S(2)}, u32[]{:S(2)}) %collective-permute-start.1) | collective-permute-done | bytes 147488 | tf_op jit(solution)/shard_map/ppermute | solution.py:123
  222.6 6.4 %collective-permute-done.2 = f32[128,288]{0,1:T(8,128)S(1)} collective-permute-done((f32[128,288]{0,1:T(8,128)S(1)}, f32[128,288]{0,1:T(8,128)S(1)}, u32[]{:S(2)}, u32[]{:S(2)}) %collective-permute-start.2) | collective-permute-done | bytes 147488 | tf_op jit(solution)/shard_map/ppermute | solution.py:123
  228.9 6.4 %collective-permute-done.3 = f32[128,288]{0,1:T(8,128)S(1)} collective-permute-done((f32[128,288]{0,1:T(8,128)S(1)}, f32[128,288]{0,1:T(8,128)S(1)}, u32[]{:S(2)}, u32[]{:S(2)}) %collective-permute-start.3) | collective-permute-done | bytes 147488 | tf_op jit(solution)/shard_map/ppermute | solution.py:123
  235.3 6.4 %collective-permute-done.4 = f32[128,288]{0,1:T(8,128)S(1)} collective-permute-done((f32[128,288]{0,1:T(8,128)S(1)}, f32[128,288]{0,1:T(8,128)S(1)}, u32[]{:S(2)}, u32[]{:S(2)}) %collective-permute-start.4) | collective-permute-done | bytes 147488 | tf_op jit(solution)/shard_map/ppermute | solution.py:123
  241.7 3.3 %convolution_bitcast_fusion.1 = f32[128,32,64]{0,2,1:T(8,128)S(1)} fusion(f32[32,128]{1,0:T(8,128)S(1)} %bitcast.165, f32[32,128]{1,0:T(8,128)S(1)} %bitcast.159, f32[128,128]{0,1:T(8,128)S(1)} %copy-done.15, pred[128,128]{0,1:T(8,128)(4,1)S(1)} %copy-done.19, bf16[4,128,32,64]{1,3,2,0:T(8,128)(2,1)} %bitcast.145, s32[]{:T(128)S(6)} %select_n.96), kind=kOutput, calls=%fused_computation.17 | convolution fusion | flops 70254592 | bytes 1703940 | tf_op jit(solution)/shard_map/hts,shp->thp/dot_general | solution.py:89
  245.0 3.0 %collective-permute-done.5 = f32[128,288]{0,1:T(8,128)S(1)} collective-permute-done((f32[128,288]{0,1:T(8,128)S(1)}, f32[128,288]{0,1:T(8,128)S(1)}, u32[]{:S(2)}, u32[]{:S(2)}) %collective-permute-start.5) | collective-permute-done | bytes 147488 | tf_op jit(solution)/shard_map/ppermute | solution.py:123
  248.0 1.1 fusion.7
  249.1 1.0 copy.65
  250.1 4.3 %collective-permute-done.6 = f32[128,288]{0,1:T(8,128)S(1)} collective-permute-done((f32[128,288]{0,1:T(8,128)S(1)}, f32[128,288]{0,1:T(8,128)S(1)}, u32[]{:S(2)}, u32[]{:S(2)}) %collective-permute-start.6) | collective-permute-done | bytes 147488 | tf_op jit(solution)/shard_map/ppermute | solution.py:123
  254.7 0.1 dynamic-slice_multiply_fusion
  254.9 1.4 copy.66
  (97 shorter events, 0.7 us)
Async XLA Ops:
  7.2 55.4 %copy-start = (bf16[128,2304]{1,0:T(8,128)(2,1)S(1)}, bf16[128,2304]{1,0:T(8,128)(2,1)}, u32[]{:S(2)}) copy-start(bf16[128,2304]{1,0:T(8,128)(2,1)} %param.11) | copy-start | bytes 1769476
  7.2 119.1 %all-gather.4.cloned.1.call-start = ((), (), s32[]{:S(2)}) async-start(), calls=%async_computation.3 | async-start | bytes 5242880 | tf_op jit(solution)/shard_map/all_gather | solution.py:79
  9.8 54.3 %copy-start.25 = (f32[128]{0:T(128)}, f32[128]{0:T(128)S(1)}, u32[]{:S(2)}) copy-start(f32[128]{0:T(128)S(1)} %add_multiply_fusion) | copy-start | bytes 1540
  62.4 1.7 copy-start.29
  62.5 1.7 copy-start.30
  62.5 3.0 %copy-start.27 = (f32[32]{0:T(128)S(1)}, f32[32]{0:T(128)}, u32[]{:S(2)}) copy-start(f32[32]{0:T(128)} %param.14) | copy-start | bytes 388
  62.5 2.8 %copy-start.20 = (f32[512,1]{0,1:T(1,128)}, f32[512,1]{0,1:T(1,128)S(1)}, u32[]{:S(2)}) copy-start(f32[512,1]{0,1:T(1,128)S(1)} %fusion.89) | copy-start | bytes 6148
  64.2 13.2 %copy-start.1 = (bf16[512,2304]{1,0:T(8,128)(2,1)}, bf16[512,2304]{1,0:T(8,128)(2,1)S(1)}, u32[]{:S(2)}) copy-start(bf16[512,2304]{1,0:T(8,128)(2,1)S(1)} %convolution_convert_fusion) | copy-start | bytes 7077892
  67.4 11.6 %copy-start.7 = (f32[4,128,32]{2,1,0:T(8,128)}, f32[4,128,32]{2,1,0:T(8,128)S(1)}, u32[]{:S(2)}) copy-start(f32[4,128,32]{2,1,0:T(8,128)S(1)} %reduce_window_sum.35) | copy-start | bytes 196612
  74.3 0.8 copy-start.4
  77.1 89.3 %reduce-scatter.2.cloned.1.call-start = ((), (), s32[]{:S(2)}) async-start(), calls=%async_computation.1 | async-start | bytes 1327104 | tf_op jit(solution)/shard_map/reduce_scatter | solution.py:119
  79.6 12.6 %copy-start.6 = (bf16[1,128,2048]{1,2,0:T(8,128)(2,1)S(1)}, bf16[1,128,2048]{1,2,0:T(8,128)(2,1)}, u32[]{:S(2)}) copy-start(bf16[1,128,2048]{1,2,0:T(8,128)(2,1)} %copy.61) | copy-start | bytes 1572868
  82.8 11.7 %copy-start.2 = (bf16[4,128,2048]{1,2,0:T(8,128)(2,1)}, bf16[4,128,2048]{1,2,0:T(8,128)(2,1)S(1)}, u32[]{:S(2)}) copy-start(bf16[4,128,2048]{1,2,0:T(8,128)(2,1)S(1)} %copy.54) | copy-start | bytes 6291460
  89.8 7.4 %copy-start.16 = (f32[1,128,32]{1,0,2:T(1,128)}, f32[1,128,32]{1,0,2:T(1,128)S(1)}, u32[]{:S(2)}) copy-start(f32[1,128,32]{1,0,2:T(1,128)S(1)} %constant_dynamic-slice_fusion.2) | copy-start | bytes 49156
  89.8 7.4 %copy-start.18 = (pred[128,128]{0,1:T(8,128)(4,1)}, pred[128,128]{0,1:T(8,128)(4,1)S(1)}, u32[]{:S(2)}) copy-start(pred[128,128]{0,1:T(8,128)(4,1)S(1)} %iota_compare_fusion) | copy-start | bytes 49156
  90.7 6.4 %copy-start.14 = (f32[128,128]{0,1:T(8,128)}, f32[128,128]{0,1:T(8,128)S(1)}, u32[]{:S(2)}) copy-start(f32[128,128]{0,1:T(8,128)S(1)} %fusion.64) | copy-start | bytes 196612
  92.2 5.0 %copy-start.12 = (f32[1,128,32]{1,2,0:T(8,128)S(1)}, f32[1,128,32]{1,2,0:T(8,128)}, u32[]{:S(2)}) copy-start(f32[1,128,32]{1,2,0:T(8,128)} %copy.57) | copy-start | bytes 49156
  97.2 2.4 copy-start.3
  100.3 26.0 %copy-start.21 = (f32[32]{0:T(128)S(1)}, f32[32]{0:T(128)}, u32[]{:S(2)}) copy-start(f32[32]{0:T(128)} %get-tuple-element.14) | copy-start | bytes 388
  100.3 26.0 %copy-start.22 = (f32[32]{0:T(128)S(1)}, f32[32]{0:T(128)}, u32[]{:S(2)}) copy-start(f32[32]{0:T(128)} %get-tuple-element.15) | copy-start | bytes 388
  100.3 26.0 %copy-start.23 = (f32[32]{0:T(128)S(1)}, f32[32]{0:T(128)}, u32[]{:S(2)}) copy-start(f32[32]{0:T(128)} %get-tuple-element.16) | copy-start | bytes 388
  100.3 26.0 %copy-start.24 = (f32[32]{0:T(128)S(1)}, f32[32]{0:T(128)}, u32[]{:S(2)}) copy-start(f32[32]{0:T(128)} %get-tuple-element.17) | copy-start | bytes 388
  126.3 3.7 %copy-start.10 = (f32[128,128]{0,1:T(8,128)S(1)}, f32[128,128]{0,1:T(8,128)}, u32[]{:S(2)}) copy-start(f32[128,128]{0,1:T(8,128)} %fusion.66) | copy-start | bytes 196612
  126.3 4.0 %copy-start.8 = (f32[128,32,64]{0,2,1:T(8,128)S(1)}, f32[128,32,64]{0,2,1:T(8,128)}, u32[]{:S(2)}) copy-start(f32[128,32,64]{0,2,1:T(8,128)} %convolution_bitcast_fusion) | copy-start | bytes 3145732
  126.3 4.0 %copy-start.11 = (f32[1,128,32]{1,2,0:T(8,128)S(1)}, f32[1,128,32]{1,2,0:T(8,128)}, u32[]{:S(2)}) copy-start(f32[1,128,32]{1,2,0:T(8,128)} %copy.64) | copy-start | bytes 49156
  129.9 1.5 copy-start.5
  129.9 1.9 copy-start.26
  129.9 1.9 copy-start.28
  131.4 110.3 %copy-start.13 = (f32[1,128,32]{1,2,0:T(8,128)S(1)}, f32[1,128,32]{1,2,0:T(8,128)}, u32[]{:S(2)}) copy-start(f32[1,128,32]{1,2,0:T(8,128)} %copy.57) | copy-start | bytes 49156
  131.4 110.3 %copy-start.15 = (f32[128,128]{0,1:T(8,128)S(1)}, f32[128,128]{0,1:T(8,128)}, u32[]{:S(2)}) copy-start(f32[128,128]{0,1:T(8,128)} %copy-done.14) | copy-start | bytes 196612
  131.4 110.2 %copy-start.17 = (f32[1,128,32]{1,0,2:T(1,128)S(1)}, f32[1,128,32]{1,0,2:T(1,128)}, u32[]{:S(2)}) copy-start(f32[1,128,32]{1,0,2:T(1,128)} %copy-done.16) | copy-start | bytes 49156
  131.4 110.2 %copy-start.19 = (pred[128,128]{0,1:T(8,128)(4,1)S(1)}, pred[128,128]{0,1:T(8,128)(4,1)}, u32[]{:S(2)}) copy-start(pred[128,128]{0,1:T(8,128)(4,1)} %copy-done.18) | copy-start | bytes 49156
  133.4 76.2 %all-reduce.2.cloned.1.call-start = ((), (), s32[]{:S(2)}) async-start(), calls=%async_computation.2 | async-start | bytes 294912 | tf_op jit(solution)/shard_map/psum | solution.py:120
  209.6 6.6 %collective-permute-start = (f32[128,288]{0,1:T(8,128)}, f32[128,288]{0,1:T(8,128)S(1)}, u32[]{:S(2)}, u32[]{:S(2)}) collective-permute-start(f32[128,288]{0,1:T(8,128)} %all-reduce.2.cloned.1.call-done), channel_id=1, source_target_pairs={{0,1},{1,2},{2,3},{3,4},{4,5},{5,6},{6,7},{7,0},{8,9},{9,10},{10,1... | collective-permute-start | bytes 442376 | tf_op jit(solution)/shard_map/ppermute | solution.py:123
  216.2 6.4 %collective-permute-start.1 = (f32[128,288]{0,1:T(8,128)S(1)}, f32[128,288]{0,1:T(8,128)S(1)}, u32[]{:S(2)}, u32[]{:S(2)}) collective-permute-start(f32[128,288]{0,1:T(8,128)S(1)} %collective-permute-done), channel_id=1, source_target_pairs={{0,1},{1,2},{2,3},{3,4},{4,5},{5,6},{6,7},{7,0},{8,9},{9,10},{10,1... | collective-permute-start | bytes 442376 | tf_op jit(solution)/shard_map/ppermute | solution.py:123
  222.6 6.4 %collective-permute-start.2 = (f32[128,288]{0,1:T(8,128)S(1)}, f32[128,288]{0,1:T(8,128)S(1)}, u32[]{:S(2)}, u32[]{:S(2)}) collective-permute-start(f32[128,288]{0,1:T(8,128)S(1)} %collective-permute-done.1), channel_id=1, source_target_pairs={{0,1},{1,2},{2,3},{3,4},{4,5},{5,6},{6,7},{7,0},{8,9},{9,10},{10,1... | collective-permute-start | bytes 442376 | tf_op jit(solution)/shard_map/ppermute | solution.py:123
  228.9 6.4 %collective-permute-start.3 = (f32[128,288]{0,1:T(8,128)S(1)}, f32[128,288]{0,1:T(8,128)S(1)}, u32[]{:S(2)}, u32[]{:S(2)}) collective-permute-start(f32[128,288]{0,1:T(8,128)S(1)} %collective-permute-done.2), channel_id=1, source_target_pairs={{0,1},{1,2},{2,3},{3,4},{4,5},{5,6},{6,7},{7,0},{8,9},{9,10},{10,1... | collective-permute-start | bytes 442376 | tf_op jit(solution)/shard_map/ppermute | solution.py:123
  235.3 6.4 %collective-permute-start.4 = (f32[128,288]{0,1:T(8,128)S(1)}, f32[128,288]{0,1:T(8,128)S(1)}, u32[]{:S(2)}, u32[]{:S(2)}) collective-permute-start(f32[128,288]{0,1:T(8,128)S(1)} %collective-permute-done.3), channel_id=1, source_target_pairs={{0,1},{1,2},{2,3},{3,4},{4,5},{5,6},{6,7},{7,0},{8,9},{9,10},{10,1... | collective-permute-start | bytes 442376 | tf_op jit(solution)/shard_map/ppermute | solution.py:123
  241.7 6.4 %collective-permute-start.5 = (f32[128,288]{0,1:T(8,128)S(1)}, f32[128,288]{0,1:T(8,128)S(1)}, u32[]{:S(2)}, u32[]{:S(2)}) collective-permute-start(f32[128,288]{0,1:T(8,128)S(1)} %collective-permute-done.4), channel_id=1, source_target_pairs={{0,1},{1,2},{2,3},{3,4},{4,5},{5,6},{6,7},{7,0},{8,9},{9,10},{10,1... | collective-permute-start | bytes 442376 | tf_op jit(solution)/shard_map/ppermute | solution.py:123
  245.0 9.6 %copy-start.9 = (f32[128,288]{0,1:T(8,128)S(1)}, f32[128,288]{0,1:T(8,128)}, u32[]{:S(2)}) copy-start(f32[128,288]{0,1:T(8,128)} %all-reduce.2.cloned.1.call-done) | copy-start | bytes 442372
  248.0 6.4 %collective-permute-start.6 = (f32[128,288]{0,1:T(8,128)S(1)}, f32[128,288]{0,1:T(8,128)S(1)}, u32[]{:S(2)}, u32[]{:S(2)}) collective-permute-start(f32[128,288]{0,1:T(8,128)S(1)} %collective-permute-done.5), channel_id=1, source_target_pairs={{0,1},{1,2},{2,3},{3,4},{4,5},{5,6},{6,7},{7,0},{8,9},{9,10},{10,1... | collective-permute-start | bytes 442376 | tf_op jit(solution)/shard_map/ppermute | solution.py:123
Sparse Core Ops, SparseCore 0:
  77.2 48.9 all-gather.3
  133.6 32.8 reduce-scatter.1
  169.3 40.2 all-reduce.1
